TPU v7x, 32 devices: a whole 2x2x4 slice. The times are simulated.
32 devices in a mesh: wl: 2 (over y), row: 16 (over z, x, core).
Axes of the slice: x: 2, y: 2, z: 4, core: 2. Of those that a mesh axis runs over, the one named last changes fastest.
Arguments:
- scenes: float32 [2, 4096, 4096], P(None, 'row'), may hold values from -6 to 6
- optics: bfloat16 [4, 2, 4096, 4096], P('wl', None, 'row'), may hold values from -4 to 4
- weights: float32 [4, 2], replicated, may hold values from 0.1 to 2
Outputs:
- blurred: float32 [2, 4096, 4096], P(None, 'row', 'wl')
All inputs are finite; a program needn't handle non-finite values.
Results may differ from a plain program's by a relative error of at most 0.0003.
Values may be sent and summed in bfloat16 or wider, within the bound.
No kernel may reach another device: no remote copies, remote signals or barrier semaphores. Data moves between devices by JAX's collectives and lax.ppermute only.
A program may use at most 128 MiB of HBM per device.

v0:
```python
import math
import jax
import jax.numpy as jnp
from jax import lax
from jax.sharding import PartitionSpec as P

PRECISE = lax.Precision.HIGHEST
NARROW = 32


def phase(left_ids, right_ids, modulus, orient):
    turns = (left_ids * right_ids % modulus).astype(jnp.float32)
    angles = turns * (orient * 2.0 * math.pi / modulus)
    return (jnp.cos(angles), jnp.sin(angles))


def ids(count):
    return jnp.arange(count, dtype=jnp.int32)


def cblock(cos_part, sin_part):
    return jnp.stack([jnp.stack([cos_part, -sin_part]), jnp.stack([sin_part, cos_part])])


def small_tables(out_count, in_count, modulus, orients):
    tables = []
    for orient in orients:
        cos_part, sin_part = phase(ids(out_count)[:, None], ids(in_count)[None, :], modulus, orient)
        tables.append(cblock(cos_part, sin_part))
    return jnp.stack(tables)


def twist(values, axis_e, cos_part, sin_part):
    real = jnp.take(values, 0, axis=axis_e)
    imag = jnp.take(values, 1, axis=axis_e)
    return jnp.stack([real * cos_part - imag * sin_part, real * sin_part + imag * cos_part], axis_e)


def canon_to_groups(canon, group_count):
    mcount, span_c = (canon.shape[0], canon.shape[-1] // 2)
    mid = canon.shape[1:-1]
    if group_count == mcount:
        return canon
    span = mcount * span_c // group_count
    flat = jnp.moveaxis(canon.reshape((mcount,) + mid + (2, span_c)), 0, -2)
    flat = flat.reshape(mid + (2, group_count, span))
    return jnp.moveaxis(flat, -2, 0).reshape((group_count,) + mid + (2 * span,))


def groups_to_canon(grouped, mcount, axis_g):
    group_count = grouped.shape[axis_g]
    if group_count == mcount:
        return grouped
    moved = jnp.moveaxis(grouped, axis_g, 0)
    mid = moved.shape[1:-1]
    span = moved.shape[-1] // 2
    span_c = group_count * span // mcount
    flat = jnp.moveaxis(moved.reshape((group_count,) + mid + (2, span)), 0, -2)
    flat = flat.reshape(mid + (2, mcount, span_c))
    canon = jnp.moveaxis(flat, -2, 0).reshape((mcount,) + mid + (2 * span_c,))
    return jnp.moveaxis(canon, 0, axis_g)


def forward_rows(scenes):
    rows_here, length = (scenes.shape[1], scenes.shape[2])
    across = length // NARROW
    half_k = across // 2
    grid = scenes.reshape((2, rows_here, NARROW, across))
    first_tab = jnp.transpose(small_tables(NARROW, NARROW, NARROW, (-1.0, 1.0)), (0, 3, 1, 2, 4))
    first = jnp.einsum("oaedb,drbn->oaern", first_tab, grid, precision=PRECISE)
    tw_cos, tw_sin = ([], [])
    for orient in (-1.0, 1.0):
        cos_part, sin_part = phase(ids(NARROW)[:, None], ids(across)[None, :], length, orient)
        tw_cos.append(cos_part)
        tw_sin.append(sin_part)
    tw_cos = jnp.stack(tw_cos)[:, :, None, :]
    tw_sin = jnp.stack(tw_sin)[:, :, None, :]
    turned = twist(first, 2, tw_cos, tw_sin)
    second_tab = jnp.transpose(small_tables(half_k, across, across, (-1.0, 1.0)), (0, 2, 4, 1, 3))
    second = jnp.einsum("oaern,oenfk->oarfk", turned, second_tab, precision=PRECISE)
    signs = 1.0 - 2.0 * (ids(across) % 2).astype(jnp.float32)
    nyquist = jnp.einsum("ern,n->er", first[0, 0], signs, precision=PRECISE)
    per_block = across // NARROW
    mcount = half_k // per_block
    blocks = second.reshape((2, NARROW, rows_here, 2, mcount, per_block))
    canon = jnp.transpose(blocks, (4, 3, 2, 0, 5, 1)).reshape((mcount, 2, rows_here, 2 * across))
    canon = canon.at[0, :, :, across].set(nyquist)
    return canon


def forward_cols(columns):
    length, width = (columns.shape[1], columns.shape[2])
    across = length // NARROW
    grid = columns.reshape((2, NARROW, across, width))
    first_tab = jnp.transpose(small_tables(NARROW, NARROW, NARROW, (-1.0, 1.0)), (0, 3, 1, 2, 4))
    first = jnp.einsum("oafeb,ebnj->oafnj", first_tab, grid, precision=PRECISE)
    tw_cos, tw_sin = ([], [])
    for orient in (-1.0, 1.0):
        cos_part, sin_part = phase(ids(NARROW)[:, None], ids(across)[None, :], length, orient)
        tw_cos.append(cos_part)
        tw_sin.append(sin_part)
    tw_cos = jnp.stack(tw_cos)[:, :, :, None]
    tw_sin = jnp.stack(tw_sin)[:, :, :, None]
    turned = twist(first, 2, tw_cos, tw_sin)
    second_tab = small_tables(across, across, across, (-1.0, 1.0))
    second = jnp.einsum("ofekn,oaenj->ofkaj", second_tab, turned, precision=PRECISE)
    return second.reshape((2, 2, length, width))


def inverse_cols_half(combined, group_count, half_index, part=0, parts=1):
    length, width = (combined.shape[1], combined.shape[2])
    across = length // NARROW
    grid = combined.reshape((2, NARROW, across, width))
    first_tab = jnp.transpose(small_tables(NARROW, NARROW, NARROW, (1.0,))[0], (2, 0, 1, 3))
    first = jnp.einsum("afeb,ebnj->afnj", first_tab, grid, precision=PRECISE)
    cos_part, sin_part = phase(ids(NARROW)[:, None], ids(across)[None, :], length, 1.0)
    turned = twist(first, 1, cos_part[:, :, None], sin_part[:, :, None])
    per_group = across // group_count
    per_half = per_group // 2
    per_part = per_half // parts
    k_ids = ids(per_part)[None, :] + part * per_part
    k_ids = ids(group_count)[:, None] * per_group + half_index * per_half + k_ids
    cos_k, sin_k = phase(k_ids.reshape((-1, 1)), ids(across)[None, :], across, 1.0)
    second_tab = jnp.transpose(cblock(cos_k, sin_k), (0, 2, 1, 3))
    second = jnp.einsum("fken,aenj->fkaj", second_tab, turned, precision=PRECISE)
    return second.reshape((2, group_count, per_part * NARROW, width))


def inverse_cols(combined):
    length, width = (combined.shape[1], combined.shape[2])
    across = length // NARROW
    grid = combined.reshape((2, NARROW, across, width))
    first_tab = jnp.transpose(small_tables(NARROW, NARROW, NARROW, (1.0,))[0], (2, 0, 1, 3))
    first = jnp.einsum("afeb,ebnj->afnj", first_tab, grid, precision=PRECISE)
    cos_part, sin_part = phase(ids(NARROW)[:, None], ids(across)[None, :], length, 1.0)
    turned = twist(first, 1, cos_part[:, :, None], sin_part[:, :, None])
    second_tab = jnp.transpose(small_tables(across, across, across, (1.0,))[0], (0, 2, 1, 3))
    second = jnp.einsum("fken,aenj->fkaj", second_tab, turned, precision=PRECISE)
    return second.reshape((2, length, width))


def inverse_rows(canon, length, scale, k_count=None, k_start=0):
    mcount, rows_here, width = (canon.shape[1], canon.shape[2], canon.shape[3])
    across = width // 2
    k_count = across if k_count is None else k_count
    first_tab = jnp.transpose(small_tables(NARROW, mcount, NARROW, (1.0, -1.0)), (0, 3, 1, 2, 4))
    first = jnp.einsum("oafem,emRj->oafRj", first_tab, canon, precision=PRECISE)
    lower = first[0, :, :, :, :across]
    upper = first[1, :, :, :, across:]
    flip_gain = -2.0 * (ids(NARROW) % 2).astype(jnp.float32)
    fix = flip_gain[:, None, None] * canon[:, 0, :, across][None]
    lane0 = (ids(across) == 0)[None, None, None, :]
    upper = jnp.where(lane0, upper + fix[..., None], upper)
    cos_up, sin_up = phase(ids(NARROW)[:, None], ids(across)[None, :], length, 1.0)
    cos_dn, sin_dn = phase(ids(NARROW)[:, None], ids(across)[None, :], length, -1.0)
    lower = twist(lower, 1, cos_up[:, None, :], sin_up[:, None, :])
    upper = twist(upper, 1, cos_dn[:, None, :], sin_dn[:, None, :])
    tabs = []
    for orient in (1.0, -1.0):
        k_ids = ids(k_count)[:, None] + k_start
        cos_part, sin_part = phase(k_ids, ids(across)[None, :], across, orient)
        tabs.append(cblock(cos_part, sin_part))
    tabs = jnp.transpose(jnp.stack(tabs) * scale, (0, 2, 4, 1, 3))
    out = jnp.einsum("aeRu,eufk->aRfk", lower, tabs[0], precision=PRECISE)
    out = out + jnp.einsum("aeRu,eufk->aRfk", upper, tabs[1], precision=PRECISE)
    return jnp.transpose(out, (2, 1, 3, 0)).reshape((2, rows_here, k_count * NARROW))


def pair_optics(optics):
    length = optics.shape[-1]
    across = length // NARROW
    half = length // 2
    mcount = half // across
    block = [lax.slice_in_dim(optics, across * i, across * (i + 1), axis=3) for i in range(NARROW)]
    windows = []
    for m in range(mcount):
        second = block[half // across if m == 0 else NARROW - m]
        windows.append(jnp.concatenate([block[NARROW - 1 - m], second], -1))
    windows = jnp.stack(windows)
    src = ids(2 * across)[:, None]
    dst = ids(across)[None, :]
    picker = jnp.logical_or(
        jnp.logical_and(src == across - dst, dst > 0), jnp.logical_and(src == across, dst == 0)
    ).astype(optics.dtype)
    mirrored = jnp.einsum("mwcpv,vu->mwcpu", windows, picker, preferred_element_type=jnp.float32)
    lower = jnp.stack(block[:mcount])
    return jnp.concatenate([lower, mirrored.astype(optics.dtype)], -1)


def local(scenes, optics, weights):
    row_count = lax.axis_size("row")
    length = scenes.shape[2]
    across = length // NARROW
    norm_factor = 1.0 / (float(length) * float(length))
    wl_index = lax.axis_index("wl")
    local_waves = optics.shape[0]
    weight_rows = lax.dynamic_slice_in_dim(weights, wl_index * local_waves, local_waves, 0)
    first_row = lax.axis_index("row") == 0
    wl_count = lax.axis_size("wl")
    rows_here = scenes.shape[1]
    own_rows = rows_here // wl_count
    if wl_count == 2 and own_rows * wl_count == rows_here:
        mine = lax.dynamic_slice_in_dim(scenes, wl_index * own_rows, own_rows, 1)
        canon = forward_rows(mine)
        mcount = canon.shape[0]
        sent = canon_to_groups(canon, row_count)
        got = lax.all_to_all(sent, "row", split_axis=0, concat_axis=2, tiled=True)[0]
        other = lax.ppermute(got, "wl", perm=[(0, 1), (1, 0)])
        got = got.reshape((2, row_count, own_rows, got.shape[-1]))
        other = other.reshape(got.shape)
        first_half = jnp.where(wl_index == 0, got, other)
        second_half = jnp.where(wl_index == 0, other, got)
        got = jnp.stack([first_half, second_half], 2).reshape((2, length, got.shape[-1]))
    else:
        canon = forward_rows(scenes)
        mcount = canon.shape[0]
        sent = canon_to_groups(canon, row_count)
        got = lax.all_to_all(sent, "row", split_axis=0, concat_axis=2, tiled=True)[0]
    spec = forward_cols(got)
    optic_canon = pair_optics(optics)
    optic_sent = canon_to_groups(optic_canon, row_count)
    optic_got = lax.all_to_all(optic_sent, "row", split_axis=0, concat_axis=3, tiled=True)[0]
    width = spec.shape[-1]
    span = width // 2
    lane_ids = ids(width)
    itself = jnp.logical_and(first_row, lane_ids % span == 0)
    direct = spec[0]
    flipped = spec[1]
    swapped = jnp.concatenate([flipped[..., span:], flipped[..., :span]], -1)
    partner = jnp.where(itself, flipped, swapped)
    mirror_real = partner[0]
    mirror_imag = -partner[1]
    even_real = 0.5 * (direct[0] + mirror_real)
    even_imag = 0.5 * (direct[1] + mirror_imag)
    odd_real = 0.5 * (direct[0] - mirror_real)
    odd_imag = 0.5 * (direct[1] - mirror_imag)
    combined_real = jnp.zeros_like(even_real)
    combined_imag = jnp.zeros_like(even_imag)
    for colour in range(local_waves):
        mixed_real = weight_rows[colour, 0] * even_real + weight_rows[colour, 1] * odd_real
        mixed_imag = weight_rows[colour, 0] * even_imag + weight_rows[colour, 1] * odd_imag
        resp_real = optic_got[colour, 0].astype(jnp.float32)
        resp_imag = optic_got[colour, 1].astype(jnp.float32)
        combined_real = combined_real + resp_real * mixed_real - resp_imag * mixed_imag
        combined_imag = combined_imag + resp_real * mixed_imag + resp_imag * mixed_real
    stacked = jnp.stack([combined_real, combined_imag])
    back = inverse_cols(stacked)
    if wl_count != 2 or own_rows * wl_count != rows_here:
        back = back.reshape((2, row_count, rows_here, width))
        returned = lax.all_to_all(back, "row", split_axis=1, concat_axis=1, tiled=True)
        returned = groups_to_canon(returned, mcount, 1)
        result_image = inverse_rows(returned, length, norm_factor)
        return lax.psum_scatter(result_image, "wl", scatter_dimension=2, tiled=True)
    per_group = across // row_count
    if per_group % 2 == 0 and per_group * row_count == across:
        parts = 4 if per_group % 8 == 0 else 1
        incoming = []
        for part in range(parts):
            given = inverse_cols_half(stacked, row_count, 1 - wl_index, part, parts)
            incoming.append(lax.ppermute(given, "wl", perm=[(0, 1), (1, 0)]))
        incoming = jnp.concatenate(incoming, 2)
        kept = inverse_cols_half(stacked, row_count, wl_index)
    else:
        back = back.reshape((2, row_count, 2, own_rows, width))
        kept = lax.dynamic_index_in_dim(back, wl_index, 2, keepdims=False)
        given = lax.dynamic_index_in_dim(back, 1 - wl_index, 2, keepdims=False)
        incoming = lax.ppermute(given, "wl", perm=[(0, 1), (1, 0)])
    summed = kept + incoming
    returned = lax.all_to_all(summed, "row", split_axis=1, concat_axis=1, tiled=True)
    returned = groups_to_canon(returned, mcount, 1)
    k_half = across // 2
    theirs = inverse_rows(returned, length, norm_factor, k_half, (1 - wl_index) * k_half)
    taken = lax.ppermute(theirs, "wl", perm=[(0, 1), (1, 0)])
    mine = inverse_rows(returned, length, norm_factor, k_half, wl_index * k_half)
    upper = jnp.where(wl_index == 0, mine, taken)
    lower = jnp.where(wl_index == 0, taken, mine)
    return jnp.concatenate([upper, lower], 1)


def solution(mesh):
    in_specs = (P(None, "row", None), P("wl", None, "row", None), P())
    out_specs = P(None, "row", "wl")
    return jax.shard_map(local, mesh=mesh, in_specs=in_specs, out_specs=out_specs, check_vma=False)
```

profile of v0, /device:TPU:10, one launch (start us, length us, event | category | flops | bytes accessed | tf_op | source)
XLA Modules:
  0.0 713.1 jit_solution(16438513354789603543)
XLA Ops:
  5.1 6.8 fusion.46
  15.1 13.9 %fusion.17 = f32[2,32,128,2,64,1]{2,4,5,3,1,0:T(8,128)S(1)} fusion(f32[2,32,2,128,128,1]{4,1,3,0,2,5:T(8,128)S(1)} %maximum_bitcast_fusion.1, f32[1,2,2,64,128]{4,3,2,1,0:T(8,128)S(1)} %maximum_bitcast_fusion.22, f32[1,2,2,64,128]{4,3,2,1,0:T(8,128)S(1)} %maximum_bitcast_fusion.21), kind=kOutput, calls=%fused_computation.26 | convolution fusion | flops 3221291008 | bytes 12845056 | tf_op jit(solution)/shard_map/oaern,oenfk->oarfk/dot_general | solution.py:80
  39.4 6.2 all-to-all-start.1
  98.0 7.8 %pad_maximum_fusion = bf16[16,2,2,256,256]{3,4,2,1,0:T(8,128)(2,1)} fusion(bf16[16,2,2,256,128]{3,4,2,1,0:T(8,128)(2,1)} %convolution_convert_fusion, bf16[16,2,2,256,128]{3,4,2,1,0:T(8,128)(2,1)} %bitcast_dynamic-update-slice_fusion.15), kind=kLoop, calls=%fused_computation.5 | loop fusion | flops 16777216 | bytes 16777216 | tf_op jit(solution)/shard_map/concatenate | solution.py:187
  105.9 32.1 %all-to-all-done.1 = f32[16,2,128,256]{2,3,1,0:T(8,128)} async-done(((f32[16,2,128,256]{2,3,1,0:T(8,128)}), f32[16,2,128,256]{2,3,1,0:T(8,128)}, u32[]{:S(2)}, u32[]{:S(2)}) %all-to-all-start.1) | async-done | bytes 4194336 | tf_op jit(solution)/shard_map/all_to_all | solution.py:207
  160.9 80.8 %collective-permute-done = f32[2,2048,256]{2,1,0:T(8,128)} collective-permute-done((f32[2,2048,256]{2,1,0:T(8,128)}, f32[2,2048,256]{2,1,0:T(8,128)}, u32[]{:S(2)}, u32[]{:S(2)}) %collective-permute-start) | collective-permute-done | bytes 4194336 | tf_op jit(solution)/shard_map/ppermute | solution.py:208
  255.0 13.3 %copy.175 = f32[2,16,2,128,256]{4,2,1,0,3:T(2,128)} copy(f32[2,16,2,128,256]{3,4,0,1,2:T(8,128)} %pad_maximum_fusion.1) | data formatting | bytes 16777216 | tf_op jit(solution)/shard_map/stack | solution.py:213
  268.3 10.9 %reshape.2175 = f32[2,32,128,256,1,1]{3,1,0,2,4,5:T(8,128)} reshape(f32[2,16,2,128,256]{4,2,1,0,3:T(2,128)} %copy.175) | data formatting | bytes 16777216 | tf_op jit(solution)/shard_map/reshape;reshape | solution.py:94
  279.2 16.7 %fusion.19 = f32[2,32,2,128,256]{4,1,3,2,0:T(8,128)S(1)} fusion(f32[2,32,128,256,1,1]{3,1,0,2,4,5:T(8,128)} %reshape.2175, f32[1,2,2,32,32]{4,3,2,1,0:T(8,128)S(1)} %fusion.98, f32[1,2,2,32,32]{4,3,2,1,0:T(8,128)S(1)} %maximum_bitcast_fusion.31), kind=kOutput, calls=%fused_computation.30 | convolution fusion | flops 3221233664 | bytes 25198592 | tf_op jit(solution)/shard_map/oafeb,ebnj->oafnj/dot_general | solution.py:96
  295.9 6.0 subtract_bitcast_fusion
  306.9 25.0 %fusion.22 = f32[2,2,128,32,256]{4,2,3,1,0:T(8,128)S(1)} fusion(f32[2,32,2,128,256,1]{4,1,3,0,2,5:T(8,128)S(1)} %maximum_bitcast_fusion, f32[1,2,2,128,128]{4,3,2,1,0:T(8,128)} %maximum_bitcast_fusion.12, f32[1,2,2,128,128]{4,3,2,1,0:T(8,128)} %maximum_bitcast_fusion.11), kind=kOutput, calls=%fused_computation.31 | convolution fusion | flops 12885032960 | bytes 34078720 | tf_op jit(solution)/shard_map/ofekn,oaenj->ofkaj/dot_general | solution.py:106
  331.9 5.8 copy-done.3
  342.1 8.2 %copy.181 = f32[1,2,128,32,256]{4,3,2,1,0:T(8,128)S(1)} copy(f32[1,2,128,32,256]{4,2,3,1,0:T(8,128)} %slice.369) | data formatting | bytes 16777216 | tf_op jit(solution)/shard_map/slice | solution.py:228
  367.5 11.5 %copy.166 = bf16[1,2,2,16,256,256]{5,4,3,2,1,0:T(8,128)(2,1)} copy(bf16[1,2,2,16,256,256]{4,5,2,1,3,0:T(8,128)(2,1)} %bitcast.54) | data formatting | bytes 16777216 | tf_op jit(solution)/shard_map/all_to_all | solution.py:222
  379.0 11.1 %fusion.32 = (f32[1,4096,256]{2,1,0:T(8,128)S(1)}, f32[1,4096,256]{2,1,0:T(8,128)S(1)}) fusion(bf16[2,2,4096,256]{3,2,1,0:T(8,128)(2,1)} %bitcast.577, f32[]{:T(128)} %bitcast.125, f32[]{:T(128)} %bitcast.124, f32[2,4096,256]{2,1,0:T(8,128)} %maximum_select_fusion, f32[1,1,128,32,256]{4,3,2,1,0:T(8,128)} %copy.180, f32[]{:T(128)} %bitcast.130, f32[]{:T(128)} %bitcast.129, ...), kind=kLoop, calls=%fused_computation.49 | loop fusion | flops 36700160 | bytes 33554448 | tf_op jit(solution)/shard_map/sub | solution.py:244
  395.0 7.7 %fusion.47 = f32[32,2,128,256]{3,0,2,1:T(8,128)S(1)} fusion(f32[1,32,128,256]{3,1,0,2:T(8,128)S(1)} %copy.184, f32[1,32,128,256]{3,1,0,2:T(8,128)S(1)} %copy.183, f32[1,2,32,32]{3,2,1,0:T(8,128)S(1)} %copy-done.17, f32[1,2,32,32]{3,2,1,0:T(8,128)S(1)} %copy-done.15), kind=kOutput, calls=%fused_computation.90 | convolution fusion | flops 1612713984 | bytes 16793600 | tf_op jit(solution)/shard_map/afeb,ebnj->afnj/dot_general | solution.py:115
  405.9 9.4 %fusion.57 = f32[2,16,32,256]{3,1,2,0:T(8,128)S(1)} fusion(f32[32,2,128,256]{3,0,2,1:T(8,128)S(1)} %pad_maximum_fusion.2, f32[1,2,16,128]{3,2,1,0:T(8,128)S(1)} %copy-done.25, f32[1,2,16,128]{3,2,1,0:T(8,128)S(1)} %copy-done.24), kind=kOutput, calls=%fused_computation.111 | convolution fusion | flops 805314560 | bytes 9469952 | tf_op jit(solution)/shard_map/fken,aenj->fkaj/dot_general | solution.py:125
  416.8 10.7 %fusion.60 = f32[2,16,32,256]{3,1,2,0:T(8,128)} fusion(f32[32,2,128,256]{3,0,2,1:T(8,128)S(1)} %pad_maximum_fusion.2, f32[1,2,16,128]{3,2,1,0:T(8,128)S(1)} %copy-done.27, f32[1,2,16,128]{3,2,1,0:T(8,128)S(1)} %copy-done.26), kind=kOutput, calls=%fused_computation.112 | convolution fusion | flops 805314560 | bytes 9469952 | tf_op jit(solution)/shard_map/fken,aenj->fkaj/dot_general | solution.py:125
  428.1 10.5 %fusion.63 = f32[2,16,32,256]{3,1,2,0:T(8,128)} fusion(f32[32,2,128,256]{3,0,2,1:T(8,128)S(1)} %pad_maximum_fusion.2, f32[1,2,16,128]{3,2,1,0:T(8,128)S(1)} %copy-done.29, f32[1,2,16,128]{3,2,1,0:T(8,128)S(1)} %copy-done.28), kind=kOutput, calls=%fused_computation.113 | convolution fusion | flops 805314560 | bytes 9469952 | tf_op jit(solution)/shard_map/fken,aenj->fkaj/dot_general | solution.py:125
  440.1 10.5 %fusion.66 = f32[2,16,32,256]{3,1,2,0:T(8,128)} fusion(f32[32,2,128,256]{3,0,2,1:T(8,128)S(1)} %pad_maximum_fusion.2, f32[1,2,16,128]{3,2,1,0:T(8,128)S(1)} %copy-done.31, f32[1,2,16,128]{3,2,1,0:T(8,128)S(1)} %copy-done.30), kind=kOutput, calls=%fused_computation.114 | convolution fusion | flops 805314560 | bytes 9469952 | tf_op jit(solution)/shard_map/fken,aenj->fkaj/dot_general | solution.py:125
  451.6 13.0 %fusion.48 = f32[2,64,32,256]{3,1,2,0:T(8,128)S(1)} fusion(f32[32,2,128,256]{3,0,2,1:T(8,128)} %copy-done.2, f32[1,2,64,128]{3,2,1,0:T(8,128)S(1)} %get-tuple-element.164, f32[1,2,64,128]{3,2,1,0:T(8,128)S(1)} %get-tuple-element.163), kind=kOutput, calls=%fused_computation.92 | convolution fusion | flops 3221258240 | bytes 12713984 | tf_op jit(solution)/shard_map/fken,aenj->fkaj/dot_general | solution.py:125
  467.1 19.4 %collective-permute-done.3 = f32[2,16,32,256]{3,1,2,0:T(8,128)} collective-permute-done((f32[2,16,32,256]{3,1,2,0:T(8,128)}, f32[2,16,32,256]{3,1,2,0:T(8,128)}, u32[]{:S(2)}, u32[]{:S(2)}) %collective-permute-start.3) | collective-permute-done | bytes 1048608 | tf_op jit(solution)/shard_map/ppermute | solution.py:260
  486.5 20.7 %collective-permute-done.4 = f32[2,16,32,256]{3,1,2,0:T(8,128)} collective-permute-done((f32[2,16,32,256]{3,1,2,0:T(8,128)}, f32[2,16,32,256]{3,1,2,0:T(8,128)}, u32[]{:S(2)}, u32[]{:S(2)}) %collective-permute-start.4) | collective-permute-done | bytes 1048608 | tf_op jit(solution)/shard_map/ppermute | solution.py:260
  507.2 6.0 maximum_add_fusion
  517.7 6.0 all-to-all-start.2
  524.6 91.5 %all-to-all-done.2 = f32[2,16,128,256]{3,2,0,1:T(8,128)} async-done(((f32[2,16,128,256]{3,2,0,1:T(8,128)}), f32[2,16,128,256]{3,2,0,1:T(8,128)}, u32[]{:S(2)}, u32[]{:S(2)}) %all-to-all-start.2) | async-done | bytes 4194336 | tf_op jit(solution)/shard_map/all_to_all | solution.py:269
  616.0 18.1 %convolution_bitcast_fusion = f32[2,32,2,128,256]{4,1,3,2,0:T(8,128)S(1)} fusion(f32[2,16,128,256,1,1]{3,2,0,1,5,4:T(8,128)} %bitcast.181, f32[1,2,2,32,16]{3,4,2,1,0:T(8,128)S(1)} %maximum_bitcast_fusion.45, f32[1,2,2,32,16]{3,4,2,1,0:T(8,128)S(1)} %maximum_bitcast_fusion.44), kind=kOutput, calls=%fused_computation.32 | convolution fusion | flops 1610616832 | bytes 20987904 | tf_op jit(solution)/shard_map/oafem,emRj->oafRj/dot_general | solution.py:147
  639.9 6.9 fusion.38
  646.8 7.1 fusion.51
  657.2 8.1 %fusion.40 = f32[32,128,2,64,1]{1,3,4,2,0:T(8,128)S(1)} fusion(f32[32,2,128,128,1]{3,0,2,1,4:T(8,128)} %copy-done.6, f32[2,2,128,2,64]{2,4,1,3,0:T(8,128)S(1)} %fusion.75), kind=kOutput, calls=%fused_computation.83 | convolution fusion | flops 1610612736 | bytes 6422528 | tf_op jit(solution)/shard_map/aeRu,eufk->aRfk/dot_general | solution.py:165
  665.3 6.9 fusion.52
  673.4 29.8 %collective-permute-done.5 = f32[2,128,2048]{1,2,0:T(8,128)} collective-permute-done((f32[2,128,2048]{1,2,0:T(8,128)S(1)}, f32[2,128,2048]{1,2,0:T(8,128)}, u32[]{:S(2)}, u32[]{:S(2)}) %collective-permute-start.5) | collective-permute-done | bytes 2097184 | tf_op jit(solution)/shard_map/ppermute | solution.py:273
  (248 shorter events, 170.6 us)
Async XLA Ops:
  0.0 150.5 %copy-start = (f32[4,2]{0,1:T(2,128)S(1)}, f32[4,2]{0,1:T(2,128)}, u32[]{:S(2)}) copy-start(f32[4,2]{0,1:T(2,128)} %param.23) | copy-start | bytes 100
  29.0 3.5 copy-start.35
  39.4 98.6 %all-to-all-start.1 = ((f32[16,2,128,256]{2,3,1,0:T(8,128)}), f32[16,2,128,256]{2,3,1,0:T(8,128)}, u32[]{:S(2)}, u32[]{:S(2)}) async-start(f32[16,2,128,256]{2,3,1,0:T(8,128)} %scatter.4), calls=%async_computation.1 | async-start | bytes 8388608 | tf_op jit(solution)/shard_map/all_to_all | solution.py:207
  45.7 47.5 %copy-start.32 = (pred[128]{0:T(512)(128)(4,1)}, pred[128]{0:T(512)(128)(4,1)S(1)}, u32[]{:S(2)}) copy-start(pred[128]{0:T(512)(128)(4,1)S(1)} %get-tuple-element.218) | copy-start | bytes 388
  57.3 8.8 %copy-start.8 = (bf16[2,2,256,128]{3,2,1,0:T(8,128)(2,1)S(1)}, bf16[2,2,256,128]{3,2,1,0:T(8,128)(2,1)}, u32[]{:S(2)}) copy-start(bf16[2,2,256,128]{3,2,1,0:T(8,128)(2,1)} %get-tuple-element.143) | copy-start | bytes 786436
  84.5 8.7 %copy-start.34 = (s32[128]{0:T(128)S(1)}, s32[128]{0:T(128)}, u32[]{:S(2)}) copy-start(s32[128]{0:T(128)} %iota_subtract_fusion) | copy-start | bytes 1540
  138.0 229.5 %all-to-all-start = ((bf16[16,2,2,256,256]{3,4,2,1,0:T(8,128)(2,1)}), bf16[16,2,2,256,256]{3,4,2,1,0:T(8,128)(2,1)}, u32[]{:S(2)}, u32[]{:S(2)}) async-start(bf16[16,2,2,256,256]{3,4,2,1,0:T(8,128)(2,1)} %pad_maximum_fusion), calls=%async_computation | async-start | bytes 16777216 | tf_op jit(solution)/shard_map/all_to_all | solution.py:222
  143.4 6.9 copy-start.13
  143.4 7.0 copy-start.11
  148.7 92.9 %collective-permute-start = (f32[2,2048,256]{2,1,0:T(8,128)}, f32[2,2048,256]{2,1,0:T(8,128)}, u32[]{:S(2)}, u32[]{:S(2)}) collective-permute-start(f32[2,2048,256]{2,1,0:T(8,128)} %bitcast.586), channel_id=1, source_target_pairs={{0,16},{16,0},{1,17},{17,1},{2,18},{18,2},{3,19},{19,3},{4,20},{20... | collective-permute-start | bytes 12582920 | tf_op jit(solution)/shard_map/ppermute | solution.py:208
  153.8 5.6 copy-start.20
  153.8 5.6 copy-start.22
  331.9 5.8 copy-start.3
  395.0 7.7 %copy-start.18 = (f32[32,128]{0,1:T(8,128)S(1)}, f32[32,128]{0,1:T(8,128)}, u32[]{:S(2)}) copy-start(f32[32,128]{0,1:T(8,128)} %copy.185) | copy-start | bytes 49156
  395.0 7.7 %copy-start.19 = (f32[32,128]{0,1:T(8,128)S(1)}, f32[32,128]{0,1:T(8,128)}, u32[]{:S(2)}) copy-start(f32[32,128]{0,1:T(8,128)} %copy.186) | copy-start | bytes 49156
  405.8 34.3 %copy-start.2 = (f32[32,2,128,256]{3,0,2,1:T(8,128)}, f32[32,2,128,256]{3,0,2,1:T(8,128)S(1)}, u32[]{:S(2)}) copy-start(f32[32,2,128,256]{3,0,2,1:T(8,128)S(1)} %pad_maximum_fusion.2) | copy-start | bytes 25165828
  405.9 11.0 %copy-start.26 = (f32[1,2,16,128]{3,2,1,0:T(8,128)S(1)}, f32[1,2,16,128]{3,2,1,0:T(8,128)}, u32[]{:S(2)}) copy-start(f32[1,2,16,128]{3,2,1,0:T(8,128)} %get-tuple-element.179) | copy-start | bytes 49156
  405.9 11.0 %copy-start.27 = (f32[1,2,16,128]{3,2,1,0:T(8,128)S(1)}, f32[1,2,16,128]{3,2,1,0:T(8,128)}, u32[]{:S(2)}) copy-start(f32[1,2,16,128]{3,2,1,0:T(8,128)} %get-tuple-element.180) | copy-start | bytes 49156
  415.2 51.8 %collective-permute-start.1 = (f32[2,16,32,256]{3,1,2,0:T(8,128)S(1)}, f32[2,16,32,256]{3,1,2,0:T(8,128)S(1)}, u32[]{:S(2)}, u32[]{:S(2)}) collective-permute-start(f32[2,16,32,256]{3,1,2,0:T(8,128)S(1)} %fusion.57), channel_id=1, source_target_pairs={{0,16},{16,0},{1,17},{17,1},{2,18},{18,2},{3,19},{19,3},{4,20},{20... | collective-permute-start | bytes 3145736 | tf_op jit(solution)/shard_map/ppermute | solution.py:260
  416.8 11.3 %copy-start.28 = (f32[1,2,16,128]{3,2,1,0:T(8,128)S(1)}, f32[1,2,16,128]{3,2,1,0:T(8,128)}, u32[]{:S(2)}) copy-start(f32[1,2,16,128]{3,2,1,0:T(8,128)} %get-tuple-element.181) | copy-start | bytes 49156
  416.8 11.3 %copy-start.29 = (f32[1,2,16,128]{3,2,1,0:T(8,128)S(1)}, f32[1,2,16,128]{3,2,1,0:T(8,128)}, u32[]{:S(2)}) copy-start(f32[1,2,16,128]{3,2,1,0:T(8,128)} %get-tuple-element.182) | copy-start | bytes 49156
  427.6 39.5 %collective-permute-start.2 = (f32[2,16,32,256]{3,1,2,0:T(8,128)}, f32[2,16,32,256]{3,1,2,0:T(8,128)S(1)}, u32[]{:S(2)}, u32[]{:S(2)}) collective-permute-start(f32[2,16,32,256]{3,1,2,0:T(8,128)} %fusion.60), channel_id=1, source_target_pairs={{0,16},{16,0},{1,17},{17,1},{2,18},{18,2},{3,19},{19,3},{4,20},{20... | collective-permute-start | bytes 3145736 | tf_op jit(solution)/shard_map/ppermute | solution.py:260
  428.1 12.0 %copy-start.30 = (f32[1,2,16,128]{3,2,1,0:T(8,128)S(1)}, f32[1,2,16,128]{3,2,1,0:T(8,128)}, u32[]{:S(2)}) copy-start(f32[1,2,16,128]{3,2,1,0:T(8,128)} %get-tuple-element.183) | copy-start | bytes 49156
  428.1 12.0 %copy-start.31 = (f32[1,2,16,128]{3,2,1,0:T(8,128)S(1)}, f32[1,2,16,128]{3,2,1,0:T(8,128)}, u32[]{:S(2)}) copy-start(f32[1,2,16,128]{3,2,1,0:T(8,128)} %get-tuple-element.184) | copy-start | bytes 49156
  438.6 47.9 %collective-permute-start.3 = (f32[2,16,32,256]{3,1,2,0:T(8,128)}, f32[2,16,32,256]{3,1,2,0:T(8,128)}, u32[]{:S(2)}, u32[]{:S(2)}) collective-permute-start(f32[2,16,32,256]{3,1,2,0:T(8,128)} %fusion.63), channel_id=1, source_target_pairs={{0,16},{16,0},{1,17},{17,1},{2,18},{18,2},{3,19},{19,3},{4,20},{20... | collective-permute-start | bytes 3145736 | tf_op jit(solution)/shard_map/ppermute | solution.py:260
  450.6 56.6 %collective-permute-start.4 = (f32[2,16,32,256]{3,1,2,0:T(8,128)}, f32[2,16,32,256]{3,1,2,0:T(8,128)}, u32[]{:S(2)}, u32[]{:S(2)}) collective-permute-start(f32[2,16,32,256]{3,1,2,0:T(8,128)} %fusion.66), channel_id=1, source_target_pairs={{0,16},{16,0},{1,17},{17,1},{2,18},{18,2},{3,19},{19,3},{4,20},{20... | collective-permute-start | bytes 3145736 | tf_op jit(solution)/shard_map/ppermute | solution.py:260
  517.7 98.3 %all-to-all-start.2 = ((f32[2,16,128,256]{3,2,0,1:T(8,128)}), f32[2,16,128,256]{3,2,0,1:T(8,128)}, u32[]{:S(2)}, u32[]{:S(2)}) async-start(f32[2,16,128,256]{3,2,0,1:T(8,128)} %copy.194), calls=%async_computation.2 | async-start | bytes 8388608 | tf_op jit(solution)/shard_map/all_to_all | solution.py:269
  638.8 8.1 %copy-start.4 = (f32[32,2,128,128,1]{3,0,2,1,4:T(8,128)}, f32[32,2,128,128,1]{3,0,2,1,4:T(8,128)S(1)}, u32[]{:S(2)}) copy-start(f32[32,2,128,128,1]{3,0,2,1,4:T(8,128)S(1)} %maximum_bitcast_fusion.4) | copy-start | bytes 12582916
  639.9 14.0 %copy-start.6 = (f32[32,2,128,128,1]{3,0,2,1,4:T(8,128)}, f32[32,2,128,128,1]{3,0,2,1,4:T(8,128)S(1)}, u32[]{:S(2)}) copy-start(f32[32,2,128,128,1]{3,0,2,1,4:T(8,128)S(1)} %maximum_bitcast_fusion.5) | copy-start | bytes 12582916
  655.2 48.0 %collective-permute-start.5 = (f32[2,128,2048]{1,2,0:T(8,128)S(1)}, f32[2,128,2048]{1,2,0:T(8,128)}, u32[]{:S(2)}, u32[]{:S(2)}) collective-permute-start(f32[2,128,2048]{1,2,0:T(8,128)S(1)} %bitcast.587), channel_id=1, source_target_pairs={{0,16},{16,0},{1,17},{17,1},{2,18},{18,2},{3,19},{19,3},{4,20},{20... | collective-permute-start | bytes 6291464 | tf_op jit(solution)/shard_map/ppermute | solution.py:273
  656.8 8.5 %copy-start.5 = (f32[32,2,128,128,1]{3,0,2,1,4:T(8,128)S(1)}, f32[32,2,128,128,1]{3,0,2,1,4:T(8,128)}, u32[]{:S(2)}) copy-start(f32[32,2,128,128,1]{3,0,2,1,4:T(8,128)} %copy-done.4) | copy-start | bytes 12582916
  705.1 7.7 %copy-start.1 = (f32[4,2]{0,1:T(2,128)S(1)}, f32[4,2]{0,1:T(2,128)}, u32[]{:S(2)}) copy-start(f32[4,2]{0,1:T(2,128)} %param.23) | copy-start | bytes 100
  (13 other events, 21.9 us)
where the time goes:
time: 724 us; the launch traced here: 713 us
  waiting for transfers between devices  274 us (38%)
  matrix products  178 us (25%)
  local copies, waits for them, and re-layouts  159 us (22%)
  other arithmetic  72.8 us (10%)
  starting transfers between devices  24.9 us (3%)
    all_to_all x1, waiting for transfers between devices, local(): lax.all_to_all(summed, 'row', split_axis=1, concat_axis=1, tiled=True)  91.5 us
    ppermute x1, waiting for transfers between devices, local(): other = lax.ppermute(got, 'wl', perm=[(0, 1), (1, 0)])  80.8 us
    dot_general x5, matrix products, inverse_cols_half(): jnp.einsum('fken,aenj->fkaj', second_tab, turned, precision=PRECISE)  54.1 us
    unnamed x118, local copies, waits for them, and re-layouts  48.7 us
    ppermute x4, waiting for transfers between devices, local(): incoming.append(lax.ppermute(given, 'wl', perm=[(0, 1), (1, 0)]))  40.1 us
    all_to_all x1, waiting for transfers between devices, local(): lax.all_to_all(sent, 'row', split_axis=0, concat_axis=2, tiled=True)[0]  32.1 us
    ppermute x1, waiting for transfers between devices, local(): taken = lax.ppermute(theirs, 'wl', perm=[(0, 1), (1, 0)])  29.8 us
    dot_general x1, matrix products, forward_cols(): jnp.einsum('ofekn,oaenj->ofkaj', second_tab, turned, precision=PRECISE)  25 us
  transfers between devices with their start and end apart: 9, of which 6 were waited for; matrix products, arithmetic and copies ran while one was open for 36% of the time, Pallas kernels for 0%

commit v1 on v0

--- a/solution.py
+++ b/solution.py
@@ -6,6 +6,22 @@
 
 PRECISE = lax.Precision.HIGHEST
 NARROW = 32
+
+
+def exchange_in_pairs(array, axis, split, join):
+    ways, here = (lax.axis_size(axis), lax.axis_index(axis))
+    width = array.shape[split] // ways
+    dims = list(array.shape)
+    dims[split] = width
+    height = dims[join]
+    dims[join] = height * ways
+    full = jnp.zeros(dims, array.dtype)
+    for mask in range(ways):
+        part = lax.dynamic_slice_in_dim(array, (here ^ mask) * width, width, axis=split)
+        if mask:
+            part = lax.ppermute(part, axis, [(d, d ^ mask) for d in range(ways)])
+        full = lax.dynamic_update_slice_in_dim(full, part, (here ^ mask) * height, axis=join)
+    return full
 
 
 def phase(left_ids, right_ids, modulus, orient):
@@ -266,7 +282,7 @@
         given = lax.dynamic_index_in_dim(back, 1 - wl_index, 2, keepdims=False)
         incoming = lax.ppermute(given, "wl", perm=[(0, 1), (1, 0)])
     summed = kept + incoming
-    returned = lax.all_to_all(summed, "row", split_axis=1, concat_axis=1, tiled=True)
+    returned = exchange_in_pairs(summed, "row", 1, 1)
     returned = groups_to_canon(returned, mcount, 1)
     k_half = across // 2
     theirs = inverse_rows(returned, length, norm_factor, k_half, (1 - wl_index) * k_half)

time: 724 us -> 739 us (1.021)
  local copies, waits for them, and re-layouts: 159 us -> 192 us
  waiting for transfers between devices: 274 us -> 245 us
  starting transfers between devices: 24.9 us -> 34.4 us
    all_to_all x1 -> x0, waiting for transfers between devices: 91.5 us -> none  [local(): lax.all_to_all(summed, 'row', split_axis=1, concat_axis=1, tiled=True)]
    ppermute x0 -> x15, waiting for transfers between devices: none -> 65.1 us  [exchange_in_pairs(): part = lax.ppermute(part, axis, [(d, d ^ mask) for d in range(ways)])]
    dynamic_update_slice x0 -> x17, local copies, waits for them, and re-layouts: none -> 17.1 us  [exchange_in_pairs(): lax.dynamic_update_slice_in_dim(full, part, (here ^ mask) * height, axis=...]
    ppermute x0 -> x15, starting transfers between devices: none -> 15.9 us  [exchange_in_pairs(): part = lax.ppermute(part, axis, [(d, d ^ mask) for d in range(ways)])]
    ppermute x0 -> x15, local copies, waits for them, and re-layouts: none -> 11.7 us  [exchange_in_pairs(): part = lax.ppermute(part, axis, [(d, d ^ mask) for d in range(ways)])]
    unnamed x118 -> x136, local copies, waits for them, and re-layouts: 48.7 us -> 49 us
  transfers between devices with their start and end apart: 9 -> 23, of which waited for: 6 -> 14; matrix products, arithmetic and copies ran while one was open for 36% -> 40% of each run, Pallas kernels for 0% -> 0%
where the time goes in v1:
time: 739 us; the launch traced here: 726 us
  waiting for transfers between devices  245 us (33%)
  local copies, waits for them, and re-layouts  192 us (26%)
  matrix products  176 us (24%)
  other arithmetic  74.4 us (10%)
  starting transfers between devices  34.4 us (5%)
    ppermute x1, waiting for transfers between devices, local(): other = lax.ppermute(got, 'wl', perm=[(0, 1), (1, 0)])  78 us
    ppermute x15, waiting for transfers between devices, exchange_in_pairs(): part = lax.ppermute(part, axis, [(d, d ^ mask) for d in range(ways)])  65.1 us
    dot_general x5, matrix products, inverse_cols_half(): jnp.einsum('fken,aenj->fkaj', second_tab, turned, precision=PRECISE)  54.1 us
    unnamed x136, local copies, waits for them, and re-layouts  49 us
    ppermute x4, waiting for transfers between devices, local(): incoming.append(lax.ppermute(given, 'wl', perm=[(0, 1), (1, 0)]))  39.9 us
    all_to_all x1, waiting for transfers between devices, local(): lax.all_to_all(sent, 'row', split_axis=0, concat_axis=2, tiled=True)[0]  32.1 us
    ppermute x1, waiting for transfers between devices, local(): taken = lax.ppermute(theirs, 'wl', perm=[(0, 1), (1, 0)])  29.4 us
    dot_general x1, matrix products, forward_cols(): jnp.einsum('ofekn,oaenj->ofkaj', second_tab, turned, precision=PRECISE)  25.4 us
  transfers between devices with their start and end apart: 23, of which 14 were waited for; matrix products, arithmetic and copies ran while one was open for 40% of the time, Pallas kernels for 0%

profile of v1, /device:TPU:10, one launch (start us, length us, event | category | flops | bytes accessed | tf_op | source)
XLA Modules:
  0.0 726.0 jit_solution(9026867601987635477)
XLA Ops:
  5.0 6.8 fusion.45
  14.9 13.9 %fusion.17 = f32[2,32,128,2,64,1]{2,4,5,3,1,0:T(8,128)S(1)} fusion(f32[2,32,2,128,128,1]{4,1,3,0,2,5:T(8,128)S(1)} %maximum_bitcast_fusion.1, f32[1,2,2,64,128]{4,3,2,1,0:T(8,128)S(1)} %maximum_bitcast_fusion.22, f32[1,2,2,64,128]{4,3,2,1,0:T(8,128)S(1)} %maximum_bitcast_fusion.21), kind=kOutput, calls=%fused_computation.26 | convolution fusion | flops 3221291008 | bytes 12845056 | tf_op jit(solution)/shard_map/oaern,oenfk->oarfk/dot_general | solution.py:96
  39.2 6.2 all-to-all-start.1
  97.9 7.8 %pad_maximum_fusion = bf16[16,2,2,256,256]{3,4,2,1,0:T(8,128)(2,1)} fusion(bf16[16,2,2,256,128]{3,4,2,1,0:T(8,128)(2,1)} %convolution_convert_fusion, bf16[16,2,2,256,128]{3,4,2,1,0:T(8,128)(2,1)} %bitcast_dynamic-update-slice_fusion.15), kind=kLoop, calls=%fused_computation.5 | loop fusion | flops 16777216 | bytes 16777216 | tf_op jit(solution)/shard_map/concatenate | solution.py:203
  105.7 32.1 %all-to-all-done.1 = f32[16,2,128,256]{2,3,1,0:T(8,128)} async-done(((f32[16,2,128,256]{2,3,1,0:T(8,128)}), f32[16,2,128,256]{2,3,1,0:T(8,128)}, u32[]{:S(2)}, u32[]{:S(2)}) %all-to-all-start.1) | async-done | bytes 4194336 | tf_op jit(solution)/shard_map/all_to_all | solution.py:223
  163.4 78.0 %collective-permute-done = f32[2,2048,256]{2,1,0:T(8,128)} collective-permute-done((f32[2,2048,256]{2,1,0:T(8,128)}, f32[2,2048,256]{2,1,0:T(8,128)}, u32[]{:S(2)}, u32[]{:S(2)}) %collective-permute-start) | collective-permute-done | bytes 4194336 | tf_op jit(solution)/shard_map/ppermute | solution.py:224
  254.7 13.3 %copy.152 = f32[2,16,2,128,256]{4,2,1,0,3:T(2,128)} copy(f32[2,16,2,128,256]{3,4,0,1,2:T(8,128)} %pad_maximum_fusion.1) | data formatting | bytes 16777216 | tf_op jit(solution)/shard_map/stack | solution.py:229
  268.0 10.9 %reshape.2175 = f32[2,32,128,256,1,1]{3,1,0,2,4,5:T(8,128)} reshape(f32[2,16,2,128,256]{4,2,1,0,3:T(2,128)} %copy.152) | data formatting | bytes 16777216 | tf_op jit(solution)/shard_map/reshape;reshape | solution.py:110
  278.9 17.1 %fusion.19 = f32[2,32,2,128,256]{4,1,3,2,0:T(8,128)S(1)} fusion(f32[2,32,128,256,1,1]{3,1,0,2,4,5:T(8,128)} %reshape.2175, f32[1,2,2,32,32]{4,3,2,1,0:T(8,128)S(1)} %fusion.97, f32[1,2,2,32,32]{4,3,2,1,0:T(8,128)S(1)} %maximum_bitcast_fusion.31), kind=kOutput, calls=%fused_computation.30 | convolution fusion | flops 3221233664 | bytes 25198592 | tf_op jit(solution)/shard_map/oafeb,ebnj->oafnj/dot_general | solution.py:112
  306.6 25.4 %fusion.22 = f32[2,2,128,32,256]{4,2,3,1,0:T(8,128)S(1)} fusion(f32[2,32,2,128,256,1]{4,1,3,0,2,5:T(8,128)S(1)} %maximum_bitcast_fusion, f32[1,2,2,128,128]{4,3,2,1,0:T(8,128)} %maximum_bitcast_fusion.12, f32[1,2,2,128,128]{4,3,2,1,0:T(8,128)} %maximum_bitcast_fusion.11), kind=kOutput, calls=%fused_computation.31 | convolution fusion | flops 12885032960 | bytes 34078720 | tf_op jit(solution)/shard_map/ofekn,oaenj->ofkaj/dot_general | solution.py:122
  332.0 5.8 copy-done.3
  342.2 8.2 %copy.158 = f32[1,2,128,32,256]{4,3,2,1,0:T(8,128)S(1)} copy(f32[1,2,128,32,256]{4,2,3,1,0:T(8,128)} %slice.369) | data formatting | bytes 16777216 | tf_op jit(solution)/shard_map/slice | solution.py:244
  367.6 11.4 %copy.143 = bf16[1,2,2,16,256,256]{5,4,3,2,1,0:T(8,128)(2,1)} copy(bf16[1,2,2,16,256,256]{4,5,2,1,3,0:T(8,128)(2,1)} %bitcast.54) | data formatting | bytes 16777216 | tf_op jit(solution)/shard_map/all_to_all | solution.py:238
  379.0 10.8 %fusion.32 = (f32[1,4096,256]{2,1,0:T(8,128)S(1)}, f32[1,4096,256]{2,1,0:T(8,128)S(1)}) fusion(bf16[2,2,4096,256]{3,2,1,0:T(8,128)(2,1)} %bitcast.580, f32[]{:T(128)} %bitcast.125, f32[]{:T(128)} %bitcast.124, f32[2,4096,256]{2,1,0:T(8,128)} %maximum_select_fusion, f32[1,1,128,32,256]{4,3,2,1,0:T(8,128)} %copy.157, f32[]{:T(128)} %bitcast.130, f32[]{:T(128)} %bitcast.129, ...), kind=kLoop, calls=%fused_computation.49 | loop fusion | flops 36700160 | bytes 33554448 | tf_op jit(solution)/shard_map/sub | solution.py:260
  394.8 7.9 %fusion.46 = f32[32,2,128,256]{3,0,2,1:T(8,128)S(1)} fusion(f32[1,32,128,256]{3,1,0,2:T(8,128)S(1)} %copy.161, f32[1,32,128,256]{3,1,0,2:T(8,128)S(1)} %copy.160, f32[1,2,32,32]{3,2,1,0:T(8,128)S(1)} %copy-done.17, f32[1,2,32,32]{3,2,1,0:T(8,128)S(1)} %copy-done.15), kind=kOutput, calls=%fused_computation.89 | convolution fusion | flops 1612713984 | bytes 16793600 | tf_op jit(solution)/shard_map/afeb,ebnj->afnj/dot_general | solution.py:131
  405.9 9.4 %fusion.56 = f32[2,16,32,256]{3,1,2,0:T(8,128)S(1)} fusion(f32[32,2,128,256]{3,0,2,1:T(8,128)S(1)} %pad_maximum_fusion.2, f32[1,2,16,128]{3,2,1,0:T(8,128)S(1)} %copy-done.32, f32[1,2,16,128]{3,2,1,0:T(8,128)S(1)} %copy-done.31), kind=kOutput, calls=%fused_computation.110 | convolution fusion | flops 805314560 | bytes 9469952 | tf_op jit(solution)/shard_map/fken,aenj->fkaj/dot_general | solution.py:141
  416.9 10.5 %fusion.59 = f32[2,16,32,256]{3,1,2,0:T(8,128)} fusion(f32[32,2,128,256]{3,0,2,1:T(8,128)S(1)} %pad_maximum_fusion.2, f32[1,2,16,128]{3,2,1,0:T(8,128)S(1)} %copy-done.30, f32[1,2,16,128]{3,2,1,0:T(8,128)S(1)} %copy-done.29), kind=kOutput, calls=%fused_computation.111 | convolution fusion | flops 805314560 | bytes 9469952 | tf_op jit(solution)/shard_map/fken,aenj->fkaj/dot_general | solution.py:141
  427.9 10.5 %fusion.62 = f32[2,16,32,256]{3,1,2,0:T(8,128)} fusion(f32[32,2,128,256]{3,0,2,1:T(8,128)S(1)} %pad_maximum_fusion.2, f32[1,2,16,128]{3,2,1,0:T(8,128)S(1)} %copy-done.36, f32[1,2,16,128]{3,2,1,0:T(8,128)S(1)} %copy-done.35), kind=kOutput, calls=%fused_computation.112 | convolution fusion | flops 805314560 | bytes 9469952 | tf_op jit(solution)/shard_map/fken,aenj->fkaj/dot_general | solution.py:141
  439.9 10.8 %fusion.65 = f32[2,16,32,256]{3,1,2,0:T(8,128)} fusion(f32[32,2,128,256]{3,0,2,1:T(8,128)S(1)} %pad_maximum_fusion.2, f32[1,2,16,128]{3,2,1,0:T(8,128)S(1)} %copy-done.34, f32[1,2,16,128]{3,2,1,0:T(8,128)S(1)} %copy-done.33), kind=kOutput, calls=%fused_computation.113 | convolution fusion | flops 805314560 | bytes 9469952 | tf_op jit(solution)/shard_map/fken,aenj->fkaj/dot_general | solution.py:141
  451.8 13.0 %fusion.47 = f32[2,64,32,256]{3,1,2,0:T(8,128)S(1)} fusion(f32[32,2,128,256]{3,0,2,1:T(8,128)} %copy-done.2, f32[1,2,64,128]{3,2,1,0:T(8,128)S(1)} %get-tuple-element.180, f32[1,2,64,128]{3,2,1,0:T(8,128)S(1)} %get-tuple-element.179), kind=kOutput, calls=%fused_computation.91 | convolution fusion | flops 3221258240 | bytes 12713984 | tf_op jit(solution)/shard_map/fken,aenj->fkaj/dot_general | solution.py:141
  467.3 19.2 %collective-permute-done.3 = f32[2,16,32,256]{3,1,2,0:T(8,128)} collective-permute-done((f32[2,16,32,256]{3,1,2,0:T(8,128)}, f32[2,16,32,256]{3,1,2,0:T(8,128)}, u32[]{:S(2)}, u32[]{:S(2)}) %collective-permute-start.3) | collective-permute-done | bytes 1048608 | tf_op jit(solution)/shard_map/ppermute | solution.py:276
  486.5 20.8 %collective-permute-done.4 = f32[2,16,32,256]{3,1,2,0:T(8,128)} collective-permute-done((f32[2,16,32,256]{3,1,2,0:T(8,128)}, f32[2,16,32,256]{3,1,2,0:T(8,128)}, u32[]{:S(2)}, u32[]{:S(2)}) %collective-permute-start.4) | collective-permute-done | bytes 1048608 | tf_op jit(solution)/shard_map/ppermute | solution.py:276
  542.8 7.4 %collective-permute-done.10 = f32[2,1,128,256]{3,1,2,0:T(1,128)} collective-permute-done((f32[2,1,128,256]{3,1,2,0:T(1,128)S(1)}, f32[2,1,128,256]{3,1,2,0:T(1,128)}, u32[]{:S(2)}, u32[]{:S(2)}) %collective-permute-start.10) | collective-permute-done | bytes 262176 | tf_op jit(solution)/shard_map/ppermute | solution.py:22
  561.3 20.1 %collective-permute-done.13 = f32[2,1,128,256]{3,1,2,0:T(1,128)} collective-permute-done((f32[2,1,128,256]{3,1,2,0:T(1,128)S(1)}, f32[2,1,128,256]{3,1,2,0:T(1,128)}, u32[]{:S(2)}, u32[]{:S(2)}) %collective-permute-start.13) | collective-permute-done | bytes 262176 | tf_op jit(solution)/shard_map/ppermute | solution.py:22
  582.5 10.1 %collective-permute-done.14 = f32[2,1,128,256]{3,1,2,0:T(1,128)} collective-permute-done((f32[2,1,128,256]{3,1,2,0:T(1,128)S(1)}, f32[2,1,128,256]{3,1,2,0:T(1,128)}, u32[]{:S(2)}, u32[]{:S(2)}) %collective-permute-start.14) | collective-permute-done | bytes 262176 | tf_op jit(solution)/shard_map/ppermute | solution.py:22
  595.2 8.5 %collective-permute-done.15 = f32[2,1,128,256]{3,1,2,0:T(1,128)S(1)} collective-permute-done((f32[2,1,128,256]{3,1,2,0:T(1,128)S(1)}, f32[2,1,128,256]{3,1,2,0:T(1,128)S(1)}, u32[]{:S(2)}, u32[]{:S(2)}) %collective-permute-start.15) | collective-permute-done | bytes 262176 | tf_op jit(solution)/shard_map/ppermute | solution.py:22
  632.8 15.4 %convolution_bitcast_fusion = f32[2,32,2,128,256]{4,1,3,2,0:T(8,128)S(1)} fusion(f32[2,16,128,256,1,1]{3,1,0,2,5,4:T(8,128)} %copy.221, f32[1,2,2,32,16]{3,4,2,1,0:T(8,128)S(1)} %maximum_bitcast_fusion.45, f32[1,2,2,32,16]{3,4,2,1,0:T(8,128)S(1)} %copy-done.28), kind=kOutput, calls=%fused_computation.32 | convolution fusion | flops 1610616832 | bytes 20987904 | tf_op jit(solution)/shard_map/oafem,emRj->oafRj/dot_general | solution.py:163
  653.5 6.9 fusion.37
  660.4 7.1 fusion.50
  670.7 8.1 %fusion.39 = f32[32,128,2,64,1]{1,3,4,2,0:T(8,128)S(1)} fusion(f32[32,2,128,128,1]{3,0,2,1,4:T(8,128)} %copy-done.6, f32[2,2,128,2,64]{2,4,1,3,0:T(8,128)S(1)} %fusion.74), kind=kOutput, calls=%fused_computation.82 | convolution fusion | flops 1610612736 | bytes 6422528 | tf_op jit(solution)/shard_map/aeRu,eufk->aRfk/dot_general | solution.py:181
  678.8 6.9 fusion.51
  686.9 29.4 %collective-permute-done.20 = f32[2,128,2048]{1,2,0:T(8,128)} collective-permute-done((f32[2,128,2048]{1,2,0:T(8,128)S(1)}, f32[2,128,2048]{1,2,0:T(8,128)}, u32[]{:S(2)}, u32[]{:S(2)}) %collective-permute-start.20) | collective-permute-done | bytes 2097184 | tf_op jit(solution)/shard_map/ppermute | solution.py:289
  (326 shorter events, 252.3 us)
Async XLA Ops:
  0.0 143.1 %copy-start = (f32[4,2]{0,1:T(2,128)S(1)}, f32[4,2]{0,1:T(2,128)}, u32[]{:S(2)}) copy-start(f32[4,2]{0,1:T(2,128)} %param.23) | copy-start | bytes 100
  39.2 98.6 %all-to-all-start.1 = ((f32[16,2,128,256]{2,3,1,0:T(8,128)}), f32[16,2,128,256]{2,3,1,0:T(8,128)}, u32[]{:S(2)}, u32[]{:S(2)}) async-start(f32[16,2,128,256]{2,3,1,0:T(8,128)} %scatter.4), calls=%async_computation.1 | async-start | bytes 8388608 | tf_op jit(solution)/shard_map/all_to_all | solution.py:223
  45.5 47.6 %copy-start.41 = (pred[128]{0:T(512)(128)(4,1)}, pred[128]{0:T(512)(128)(4,1)S(1)}, u32[]{:S(2)}) copy-start(pred[128]{0:T(512)(128)(4,1)S(1)} %get-tuple-element.260) | copy-start | bytes 388
  105.7 37.1 %copy-start.13 = (f32[2,32,128]{2,1,0:T(8,128)S(1)}, f32[2,32,128]{2,1,0:T(8,128)}, u32[]{:S(2)}) copy-start(f32[2,32,128]{2,1,0:T(8,128)} %copy-done.12) | copy-start | bytes 98308
  105.7 37.2 %copy-start.11 = (f32[2,32,128]{2,1,0:T(8,128)S(1)}, f32[2,32,128]{2,1,0:T(8,128)}, u32[]{:S(2)}) copy-start(f32[2,32,128]{2,1,0:T(8,128)} %copy-done.10) | copy-start | bytes 98308
  137.8 229.8 %all-to-all-start = ((bf16[16,2,2,256,256]{3,4,2,1,0:T(8,128)(2,1)}), bf16[16,2,2,256,256]{3,4,2,1,0:T(8,128)(2,1)}, u32[]{:S(2)}, u32[]{:S(2)}) async-start(bf16[16,2,2,256,256]{3,4,2,1,0:T(8,128)(2,1)} %pad_maximum_fusion), calls=%async_computation | async-start | bytes 16777216 | tf_op jit(solution)/shard_map/all_to_all | solution.py:238
  148.5 92.9 %collective-permute-start = (f32[2,2048,256]{2,1,0:T(8,128)}, f32[2,2048,256]{2,1,0:T(8,128)}, u32[]{:S(2)}, u32[]{:S(2)}) collective-permute-start(f32[2,2048,256]{2,1,0:T(8,128)} %bitcast.589), channel_id=1, source_target_pairs={{0,16},{16,0},{1,17},{17,1},{2,18},{18,2},{3,19},{19,3},{4,20},{20... | collective-permute-start | bytes 12582920 | tf_op jit(solution)/shard_map/ppermute | solution.py:224
  405.8 34.0 %copy-start.2 = (f32[32,2,128,256]{3,0,2,1:T(8,128)}, f32[32,2,128,256]{3,0,2,1:T(8,128)S(1)}, u32[]{:S(2)}) copy-start(f32[32,2,128,256]{3,0,2,1:T(8,128)S(1)} %pad_maximum_fusion.2) | copy-start | bytes 25165828
  415.3 52.0 %collective-permute-start.1 = (f32[2,16,32,256]{3,1,2,0:T(8,128)S(1)}, f32[2,16,32,256]{3,1,2,0:T(8,128)S(1)}, u32[]{:S(2)}, u32[]{:S(2)}) collective-permute-start(f32[2,16,32,256]{3,1,2,0:T(8,128)S(1)} %fusion.56), channel_id=1, source_target_pairs={{0,16},{16,0},{1,17},{17,1},{2,18},{18,2},{3,19},{19,3},{4,20},{20... | collective-permute-start | bytes 3145736 | tf_op jit(solution)/shard_map/ppermute | solution.py:276
  427.3 40.0 %collective-permute-start.2 = (f32[2,16,32,256]{3,1,2,0:T(8,128)}, f32[2,16,32,256]{3,1,2,0:T(8,128)S(1)}, u32[]{:S(2)}, u32[]{:S(2)}) collective-permute-start(f32[2,16,32,256]{3,1,2,0:T(8,128)} %fusion.59), channel_id=1, source_target_pairs={{0,16},{16,0},{1,17},{17,1},{2,18},{18,2},{3,19},{19,3},{4,20},{20... | collective-permute-start | bytes 3145736 | tf_op jit(solution)/shard_map/ppermute | solution.py:276
  427.8 12.0 %copy-start.33 = (f32[1,2,16,128]{3,2,1,0:T(8,128)S(1)}, f32[1,2,16,128]{3,2,1,0:T(8,128)}, u32[]{:S(2)}) copy-start(f32[1,2,16,128]{3,2,1,0:T(8,128)} %get-tuple-element.199) | copy-start | bytes 49156
  427.8 12.0 %copy-start.34 = (f32[1,2,16,128]{3,2,1,0:T(8,128)S(1)}, f32[1,2,16,128]{3,2,1,0:T(8,128)}, u32[]{:S(2)}) copy-start(f32[1,2,16,128]{3,2,1,0:T(8,128)} %get-tuple-element.200) | copy-start | bytes 49156
  438.4 48.1 %collective-permute-start.3 = (f32[2,16,32,256]{3,1,2,0:T(8,128)}, f32[2,16,32,256]{3,1,2,0:T(8,128)}, u32[]{:S(2)}, u32[]{:S(2)}) collective-permute-start(f32[2,16,32,256]{3,1,2,0:T(8,128)} %fusion.62), channel_id=1, source_target_pairs={{0,16},{16,0},{1,17},{17,1},{2,18},{18,2},{3,19},{19,3},{4,20},{20... | collective-permute-start | bytes 3145736 | tf_op jit(solution)/shard_map/ppermute | solution.py:276
  439.9 11.6 %copy-start.20 = (f32[1,2,64,128]{3,2,1,0:T(8,128)S(1)}, f32[1,2,64,128]{3,2,1,0:T(8,128)}, u32[]{:S(2)}) copy-start(f32[1,2,64,128]{3,2,1,0:T(8,128)} %get-tuple-element.270) | copy-start | bytes 196612
  450.7 56.5 %collective-permute-start.4 = (f32[2,16,32,256]{3,1,2,0:T(8,128)}, f32[2,16,32,256]{3,1,2,0:T(8,128)}, u32[]{:S(2)}, u32[]{:S(2)}) collective-permute-start(f32[2,16,32,256]{3,1,2,0:T(8,128)} %fusion.65), channel_id=1, source_target_pairs={{0,16},{16,0},{1,17},{17,1},{2,18},{18,2},{3,19},{19,3},{4,20},{20... | collective-permute-start | bytes 3145736 | tf_op jit(solution)/shard_map/ppermute | solution.py:276
  518.3 8.2 %collective-permute-start.5 = (f32[2,1,128,256]{3,1,2,0:T(1,128)}, f32[2,1,128,256]{3,1,2,0:T(1,128)}, u32[]{:S(2)}, u32[]{:S(2)}) collective-permute-start(f32[2,1,128,256]{3,1,2,0:T(1,128)} %get-tuple-element.165), channel_id=1, source_target_pairs={{0,1},{1,0},{2,3},{3,2},{4,5},{5,4},{6,7},{7,6},{8,9},{9,8},{10,11... | collective-permute-start | bytes 786440 | tf_op jit(solution)/shard_map/ppermute | solution.py:22
  518.3 9.9 %collective-permute-start.6 = (f32[2,1,128,256]{3,1,2,0:T(1,128)}, f32[2,1,128,256]{3,1,2,0:T(1,128)}, u32[]{:S(2)}, u32[]{:S(2)}) collective-permute-start(f32[2,1,128,256]{3,1,2,0:T(1,128)} %get-tuple-element.164), channel_id=1, source_target_pairs={{0,2},{1,3},{2,0},{3,1},{4,6},{5,7},{6,4},{7,5},{8,10},{9,11},{10,... | collective-permute-start | bytes 786440 | tf_op jit(solution)/shard_map/ppermute | solution.py:22
  519.1 14.0 %collective-permute-start.7 = (f32[2,1,128,256]{3,1,2,0:T(1,128)}, f32[2,1,128,256]{3,1,2,0:T(1,128)}, u32[]{:S(2)}, u32[]{:S(2)}) collective-permute-start(f32[2,1,128,256]{3,1,2,0:T(1,128)} %get-tuple-element.163), channel_id=1, source_target_pairs={{0,3},{1,2},{2,1},{3,0},{4,7},{5,6},{6,5},{7,4},{8,11},{9,10},{10,... | collective-permute-start | bytes 786440 | tf_op jit(solution)/shard_map/ppermute | solution.py:22
  520.4 16.1 %collective-permute-start.8 = (f32[2,1,128,256]{3,1,2,0:T(1,128)}, f32[2,1,128,256]{3,1,2,0:T(1,128)}, u32[]{:S(2)}, u32[]{:S(2)}) collective-permute-start(f32[2,1,128,256]{3,1,2,0:T(1,128)} %get-tuple-element.162), channel_id=1, source_target_pairs={{0,4},{1,5},{2,6},{3,7},{4,0},{5,1},{6,2},{7,3},{8,12},{9,13},{10,... | collective-permute-start | bytes 786440 | tf_op jit(solution)/shard_map/ppermute | solution.py:22
  521.0 18.3 %collective-permute-start.9 = (f32[2,1,128,256]{3,1,2,0:T(1,128)}, f32[2,1,128,256]{3,1,2,0:T(1,128)}, u32[]{:S(2)}, u32[]{:S(2)}) collective-permute-start(f32[2,1,128,256]{3,1,2,0:T(1,128)} %get-tuple-element.161), channel_id=1, source_target_pairs={{0,5},{1,4},{2,7},{3,6},{4,1},{5,0},{6,3},{7,2},{8,13},{9,12},{10,... | collective-permute-start | bytes 786440 | tf_op jit(solution)/shard_map/ppermute | solution.py:22
  526.5 23.6 %collective-permute-start.10 = (f32[2,1,128,256]{3,1,2,0:T(1,128)S(1)}, f32[2,1,128,256]{3,1,2,0:T(1,128)}, u32[]{:S(2)}, u32[]{:S(2)}) collective-permute-start(f32[2,1,128,256]{3,1,2,0:T(1,128)S(1)} %get-tuple-element.160), channel_id=1, source_target_pairs={{0,6},{1,7},{2,4},{3,5},{4,2},{5,3},{6,0},{7,1},{8,14},{9,15},{10,... | collective-permute-start | bytes 786440 | tf_op jit(solution)/shard_map/ppermute | solution.py:22
  528.2 26.9 %collective-permute-start.11 = (f32[2,1,128,256]{3,1,2,0:T(1,128)S(1)}, f32[2,1,128,256]{3,1,2,0:T(1,128)}, u32[]{:S(2)}, u32[]{:S(2)}) collective-permute-start(f32[2,1,128,256]{3,1,2,0:T(1,128)S(1)} %get-tuple-element.159), channel_id=1, source_target_pairs={{0,7},{1,6},{2,5},{3,4},{4,3},{5,2},{6,1},{7,0},{8,15},{9,14},{10,... | collective-permute-start | bytes 786440 | tf_op jit(solution)/shard_map/ppermute | solution.py:22
  533.0 24.1 %collective-permute-start.12 = (f32[2,1,128,256]{3,1,2,0:T(1,128)S(1)}, f32[2,1,128,256]{3,1,2,0:T(1,128)}, u32[]{:S(2)}, u32[]{:S(2)}) collective-permute-start(f32[2,1,128,256]{3,1,2,0:T(1,128)S(1)} %get-tuple-element.158), channel_id=1, source_target_pairs={{0,8},{1,9},{2,10},{3,11},{4,12},{5,13},{6,14},{7,15},{8,0},{9,1},... | collective-permute-start | bytes 786440 | tf_op jit(solution)/shard_map/ppermute | solution.py:22
  536.5 44.9 %collective-permute-start.13 = (f32[2,1,128,256]{3,1,2,0:T(1,128)S(1)}, f32[2,1,128,256]{3,1,2,0:T(1,128)}, u32[]{:S(2)}, u32[]{:S(2)}) collective-permute-start(f32[2,1,128,256]{3,1,2,0:T(1,128)S(1)} %get-tuple-element.157), channel_id=1, source_target_pairs={{0,9},{1,8},{2,11},{3,10},{4,13},{5,12},{6,15},{7,14},{8,1},{9,0},... | collective-permute-start | bytes 786440 | tf_op jit(solution)/shard_map/ppermute | solution.py:22
  539.3 53.4 %collective-permute-start.14 = (f32[2,1,128,256]{3,1,2,0:T(1,128)S(1)}, f32[2,1,128,256]{3,1,2,0:T(1,128)}, u32[]{:S(2)}, u32[]{:S(2)}) collective-permute-start(f32[2,1,128,256]{3,1,2,0:T(1,128)S(1)} %get-tuple-element.156), channel_id=1, source_target_pairs={{0,10},{1,11},{2,8},{3,9},{4,14},{5,15},{6,12},{7,13},{8,2},{9,3},... | collective-permute-start | bytes 786440 | tf_op jit(solution)/shard_map/ppermute | solution.py:22
  550.1 53.6 %collective-permute-start.15 = (f32[2,1,128,256]{3,1,2,0:T(1,128)S(1)}, f32[2,1,128,256]{3,1,2,0:T(1,128)S(1)}, u32[]{:S(2)}, u32[]{:S(2)}) collective-permute-start(f32[2,1,128,256]{3,1,2,0:T(1,128)S(1)} %get-tuple-element.155), channel_id=1, source_target_pairs={{0,11},{1,10},{2,9},{3,8},{4,15},{5,14},{6,13},{7,12},{8,3},{9,2},... | collective-permute-start | bytes 786440 | tf_op jit(solution)/shard_map/ppermute | solution.py:22
  555.1 54.5 %collective-permute-start.16 = (f32[2,1,128,256]{3,1,2,0:T(1,128)S(1)}, f32[2,1,128,256]{3,1,2,0:T(1,128)S(1)}, u32[]{:S(2)}, u32[]{:S(2)}) collective-permute-start(f32[2,1,128,256]{3,1,2,0:T(1,128)S(1)} %get-tuple-element.154), channel_id=1, source_target_pairs={{0,12},{1,13},{2,14},{3,15},{4,8},{5,9},{6,10},{7,11},{8,4},{9,5},... | collective-permute-start | bytes 786440 | tf_op jit(solution)/shard_map/ppermute | solution.py:22
  557.2 58.0 %collective-permute-start.17 = (f32[2,1,128,256]{3,1,2,0:T(1,128)S(1)}, f32[2,1,128,256]{3,1,2,0:T(1,128)S(1)}, u32[]{:S(2)}, u32[]{:S(2)}) collective-permute-start(f32[2,1,128,256]{3,1,2,0:T(1,128)S(1)} %get-tuple-element.153), channel_id=1, source_target_pairs={{0,13},{1,12},{2,15},{3,14},{4,9},{5,8},{6,11},{7,10},{8,5},{9,4},... | collective-permute-start | bytes 786440 | tf_op jit(solution)/shard_map/ppermute | solution.py:22
  581.4 39.5 %collective-permute-start.18 = (f32[2,1,128,256]{3,1,2,0:T(1,128)S(1)}, f32[2,1,128,256]{3,1,2,0:T(1,128)S(1)}, u32[]{:S(2)}, u32[]{:S(2)}) collective-permute-start(f32[2,1,128,256]{3,1,2,0:T(1,128)S(1)} %get-tuple-element.152), channel_id=1, source_target_pairs={{0,14},{1,15},{2,12},{3,13},{4,10},{5,11},{6,8},{7,9},{8,6},{9,7},... | collective-permute-start | bytes 786440 | tf_op jit(solution)/shard_map/ppermute | solution.py:22
  592.7 33.1 %collective-permute-start.19 = (f32[2,1,128,256]{3,1,2,0:T(1,128)S(1)}, f32[2,1,128,256]{3,1,2,0:T(1,128)S(1)}, u32[]{:S(2)}, u32[]{:S(2)}) collective-permute-start(f32[2,1,128,256]{3,1,2,0:T(1,128)S(1)} %get-tuple-element.151), channel_id=1, source_target_pairs={{0,15},{1,14},{2,13},{3,12},{4,11},{5,10},{6,9},{7,8},{8,7},{9,6},... | collective-permute-start | bytes 786440 | tf_op jit(solution)/shard_map/ppermute | solution.py:22
  653.5 14.0 %copy-start.6 = (f32[32,2,128,128,1]{3,0,2,1,4:T(8,128)}, f32[32,2,128,128,1]{3,0,2,1,4:T(8,128)S(1)}, u32[]{:S(2)}) copy-start(f32[32,2,128,128,1]{3,0,2,1,4:T(8,128)S(1)} %maximum_bitcast_fusion.5) | copy-start | bytes 12582916
  668.7 47.7 %collective-permute-start.20 = (f32[2,128,2048]{1,2,0:T(8,128)S(1)}, f32[2,128,2048]{1,2,0:T(8,128)}, u32[]{:S(2)}, u32[]{:S(2)}) collective-permute-start(f32[2,128,2048]{1,2,0:T(8,128)S(1)} %bitcast.590), channel_id=1, source_target_pairs={{0,16},{16,0},{1,17},{17,1},{2,18},{18,2},{3,19},{19,3},{4,20},{20... | collective-permute-start | bytes 6291464 | tf_op jit(solution)/shard_map/ppermute | solution.py:289
  (36 other events, 211.7 us)
